TPU v7x, 256 devices: a whole 4x4x8 slice. The times are simulated.
256 devices in a mesh: req: 64 (over z, y, core), tp: 4 (over x).
Axes of the slice: x: 4, y: 4, z: 8, core: 2. Of those that a mesh axis runs over, the one named last changes fastest.
Arguments:
- hidden_in: bfloat16 [8192, 2048], P('req'), may hold values from -6 to 6
- attn_gain: float32 [2048], replicated, may hold values from 0.1 to 1.9
- w_query: bfloat16 [2048, 3072], P(None, 'tp'), may hold values from -0.125 to 0.125
- w_latent: bfloat16 [2048, 576], P(None, 'tp'), may hold values from -0.125 to 0.125
- kv_gain: float32 [512], replicated, may hold values from 0.1 to 1.9
- w_key_up: bfloat16 [512, 2048], P(None, 'tp'), may hold values from -0.25 to 0.25
- w_value_up: bfloat16 [512, 2048], P(None, 'tp'), may hold values from -0.25 to 0.25
- w_out: bfloat16 [2048, 2048], P('tp'), may hold values from -0.125 to 0.125
- moe_gain: float32 [2048], replicated, may hold values from 0.1 to 1.9
- w_gate: bfloat16 [64, 2048, 1408], P('req', None, 'tp'), may hold values from -0.125 to 0.125
- w_up: bfloat16 [64, 2048, 1408], P('req', None, 'tp'), may hold values from -0.125 to 0.125
- w_down: bfloat16 [64, 1408, 2048], P('req', 'tp'), may hold values from -0.15625 to 0.15625
- latent_cache: bfloat16 [2048, 64, 576], P('req'), may hold values from -3000 to 3000
- page_table: int32 [256, 8], P('req'), may hold values from 0 to 7, as said below
- cache_len: int32 [256], P('req'), may hold values from 1 to 512, 65536 in all
- parents: int32 [256, 3, 8], P('req'), may hold values from 0 to 7
- routes: int32 [8192, 6], P('req'), may hold values from 0 to 63, all different within a row; in each aligned block of 128 rows (0 to 127, 128 to 255, ...) at most 24 rows name the same one
- route_weights: float32 [8192, 6], P('req'), may hold values from 0.1 to 1
Outputs:
- layer_out: bfloat16 [8192, 2048], P('req', 'tp')
Inputs may be any that keep to these rules, and one draw needn't show every extreme that they name: `page_table`: each request's row lists the 8 pages of that request's block of the pool, each once. `routes`: each row names 6 different experts; in the rows of one index of req no expert is named more than 24 times, a bound that some block reaches.
All inputs are finite; a program needn't handle non-finite values. No bound on the sum of `cache_len` on one device may be relied on, other than what follows from the above.
Results may differ from a plain program's by a relative error of at most 0.015.
The roundings to bfloat16 on the way count: a program that leaves them out, or rounds other values in their place, can miss the bound.
Values may be sent and summed in bfloat16 or wider, within the bound.
No kernel may reach another device: no remote copies, remote signals or barrier semaphores. Data moves between devices by JAX's collectives and lax.ppermute only.
A program may use at most 128 MiB of HBM per device.

v0:
```python
import jax
import jax.numpy as jnp
from jax import lax
from jax.sharding import PartitionSpec as P

D = 2048
NOPE = 128
ROPE = 64
VDIM = 128
LATENT = 512
TOPK = 6
EXP_DEV = 1
BEAMS = 8
STEPS = 4
PAGE = 64
PAGES = 8
MOE_CHUNKS = 4
eps = 1e-06
rope_base = 50000.0


def rms_scale(values):
    return lax.rsqrt(jnp.mean(values * values, axis=-1, keepdims=True) + eps)


def rotate(values, cos_val, sin_val):
    half_rope = values.shape[-1] // 2
    first = values[..., :half_rope]
    second = values[..., half_rope:]
    return jnp.concatenate(
        [first * cos_val - second * sin_val, second * cos_val + first * sin_val], axis=-1
    )


def expert_math(arrived, gate_w, up_w, down_w):
    gate_val = jnp.einsum("nesd,edf->nesf", arrived, gate_w, preferred_element_type=jnp.float32)
    up_val = jnp.einsum("nesd,edf->nesf", arrived, up_w, preferred_element_type=jnp.float32)
    active = (jax.nn.silu(gate_val) * up_val).astype(jnp.bfloat16)
    return jnp.einsum("nesf,efd->nesd", active, down_w, preferred_element_type=jnp.float32)


def send_home(shares):
    return lax.all_to_all(shares, "req", split_axis=0, concat_axis=0, tiled=True)


def local(
    hidden_in,
    attn_gain,
    w_query,
    w_latent,
    kv_gain,
    w_key_up,
    w_value_up,
    w_out,
    moe_gain,
    w_gate,
    w_up,
    w_down,
    latent_cache,
    page_table,
    cache_len,
    parents,
    routes,
    route_weights,
):
    highest = lax.Precision.HIGHEST
    row_count = hidden_in.shape[0]
    req_local = cache_len.shape[0]
    heads_local = w_value_up.shape[1] // VDIM
    tp_count = lax.axis_size("tp")
    req_count = lax.axis_size("req")
    col_share = D // tp_count
    max_len = PAGES * PAGE
    hidden_f = hidden_in.astype(jnp.float32)
    normed = (hidden_f * rms_scale(hidden_f) * attn_gain).astype(jnp.bfloat16)
    positions = (
        cache_len.astype(jnp.float32)[:, None, None]
        + jnp.arange(STEPS, dtype=jnp.float32)[None, :, None]
        + jnp.zeros((1, 1, BEAMS), jnp.float32)
    ).reshape(row_count)
    frequency = rope_base ** (-2.0 * jnp.arange(ROPE // 2, dtype=jnp.float32) / ROPE)
    angles = positions[:, None] * frequency[None, :]
    cos_val = jnp.cos(angles)
    sin_val = jnp.sin(angles)
    queries = jnp.dot(normed, w_query, preferred_element_type=jnp.float32).reshape(
        row_count, heads_local, NOPE + ROPE
    )
    q_nope = queries[:, :, :NOPE].astype(jnp.bfloat16)
    q_rope = rotate(queries[:, :, NOPE:], cos_val[:, None, :], sin_val[:, None, :]).astype(
        jnp.bfloat16
    )
    kv_part = jnp.dot(normed, w_latent, preferred_element_type=jnp.float32)
    kv_all = lax.all_gather(kv_part, "tp", axis=1, tiled=True)
    new_lat = kv_all[:, :LATENT] * rms_scale(kv_all[:, :LATENT]) * kv_gain
    new_rope = rotate(kv_all[:, LATENT:], cos_val, sin_val)
    new_keys = jnp.concatenate([new_lat, new_rope], axis=1).astype(jnp.bfloat16)
    key_up = w_key_up.reshape(LATENT, heads_local, NOPE)
    q_lat = jnp.einsum("nhc,lhc->nhl", q_nope, key_up, preferred_element_type=jnp.float32).astype(
        jnp.bfloat16
    )
    query_key = jnp.concatenate([q_lat, q_rope], axis=2)
    pool_index = (jnp.arange(req_local, dtype=jnp.int32) * PAGES)[:, None] + page_table
    cache_keys = jnp.take(latent_cache, pool_index.reshape(-1), axis=0).reshape(
        req_local, max_len, LATENT + ROPE
    )
    live_mask = jnp.arange(max_len, dtype=jnp.int32)[None, :] < cache_len[:, None]
    score_scale = (NOPE + ROPE) ** (-0.5)
    grouped = query_key.reshape(req_local, STEPS * BEAMS * heads_local, LATENT + ROPE)
    s_cache = (
        jnp.einsum("rqd,rld->rql", grouped, cache_keys, preferred_element_type=jnp.float32)
        * score_scale
    )
    s_cache = jnp.where(live_mask[:, None, :], s_cache, -jnp.inf).reshape(
        req_local, STEPS, BEAMS, heads_local, max_len
    )
    fresh = new_keys.reshape(req_local, STEPS, BEAMS, LATENT + ROPE).astype(jnp.float32)
    parent_hot = (parents[..., None] == jnp.arange(BEAMS, dtype=jnp.int32)).astype(jnp.float32)
    identity = jnp.broadcast_to(jnp.eye(BEAMS, dtype=jnp.float32), (req_local, BEAMS, BEAMS))
    tail_rows = []
    for step_index in range(STEPS):
        lineage = identity
        pieces = [None] * STEPS
        for earlier in range(step_index, -1, -1):
            pieces[earlier] = jnp.einsum(
                "rba,rad->rbd", lineage, fresh[:, earlier], precision=highest
            )
            if earlier > 0:
                lineage = jnp.einsum(
                    "rba,rac->rbc", lineage, parent_hot[:, earlier - 1], precision=highest
                )
        for later in range(step_index + 1, STEPS):
            pieces[later] = jnp.zeros_like(pieces[0])
        tail_rows.append(jnp.stack(pieces, axis=2))
    tail_keys = jnp.stack(tail_rows, axis=1).astype(jnp.bfloat16)
    queries_tail = query_key.reshape(req_local, STEPS, BEAMS, heads_local, LATENT + ROPE)
    s_tail = (
        jnp.einsum(
            "rsbhd,rsbjd->rsbhj", queries_tail, tail_keys, preferred_element_type=jnp.float32
        )
        * score_scale
    )
    causal = jnp.arange(STEPS)[None, :] <= jnp.arange(STEPS)[:, None]
    s_tail = jnp.where(causal[None, :, None, None, :], s_tail, -jnp.inf)
    top_score = jnp.maximum(jnp.max(s_cache, axis=-1), jnp.max(s_tail, axis=-1))
    e_cache = jnp.exp(s_cache - top_score[..., None])
    e_tail = jnp.exp(s_tail - top_score[..., None])
    total = jnp.sum(e_cache, axis=-1) + jnp.sum(e_tail, axis=-1)
    p_cache = (e_cache / total[..., None]).astype(jnp.bfloat16)
    p_tail = (e_tail / total[..., None]).astype(jnp.bfloat16)
    context = jnp.einsum(
        "rsbhl,rld->rsbhd", p_cache, cache_keys[..., :LATENT], preferred_element_type=jnp.float32
    )
    context = context + jnp.einsum(
        "rsbhj,rsbjd->rsbhd", p_tail, tail_keys[..., :LATENT], preferred_element_type=jnp.float32
    )
    context = context.astype(jnp.bfloat16).reshape(row_count, heads_local, LATENT)
    value_up = w_value_up.reshape(LATENT, heads_local, VDIM)
    head_out = (
        jnp.einsum("nhl,lhv->nhv", context, value_up, preferred_element_type=jnp.float32)
        .astype(jnp.bfloat16)
        .reshape(row_count, heads_local * VDIM)
    )
    attn_part = jnp.dot(head_out, w_out, preferred_element_type=jnp.float32)
    expert_count = EXP_DEV * req_count
    capacity = min(row_count, 2 * row_count * TOPK // expert_count)
    slot_count = expert_count * capacity
    picks = routes.reshape(-1)
    pick_hot = (picks[:, None] == jnp.arange(expert_count, dtype=jnp.int32)[None, :]).astype(
        jnp.int32
    )
    before = jnp.cumsum(pick_hot, axis=0) - pick_hot
    ranks = jnp.sum(before * pick_hot, axis=1)
    slot_of = picks * capacity + ranks
    slot_hot = (slot_of[:, None] == jnp.arange(slot_count, dtype=jnp.int32)[None, :]).reshape(
        row_count, TOPK, slot_count
    )
    gather_rows = jnp.sum(slot_hot.astype(jnp.int32), axis=1).astype(jnp.bfloat16)
    weight_rows = jnp.sum(jnp.where(slot_hot, route_weights[:, :, None], 0.0), axis=1)
    tp_index = lax.axis_index("tp")
    col_start = tp_index * col_share
    attn_cols = lax.psum_scatter(attn_part, "tp", scatter_dimension=1, tiled=True)
    hidden_cols = lax.dynamic_slice_in_dim(hidden_f, col_start, col_share, 1)
    resid_cols = hidden_cols + attn_cols
    square_sum = lax.psum(jnp.sum(resid_cols * resid_cols, axis=-1, keepdims=True), "tp")
    moe_scale = lax.rsqrt(square_sum / D + eps)
    gain_cols = lax.dynamic_slice_in_dim(moe_gain, col_start, col_share, 0)
    moe_in_cols = (resid_cols * moe_scale * gain_cols).astype(jnp.bfloat16)
    placed = jnp.dot(gather_rows.T, moe_in_cols, preferred_element_type=jnp.float32).astype(
        jnp.bfloat16
    )
    placed = placed.reshape(req_count, EXP_DEV, capacity, col_share)
    chunk = capacity // MOE_CHUNKS
    returned_parts = []
    for chunk_index in range(MOE_CHUNKS):
        arrived_cols = lax.all_to_all(
            placed[:, :, chunk_index * chunk : (chunk_index + 1) * chunk],
            "req",
            split_axis=0,
            concat_axis=0,
            tiled=True,
        )
        arrived = lax.all_gather(arrived_cols, "tp", axis=3, tiled=True)
        partial_out = expert_math(arrived, w_gate, w_up, w_down)
        shares = lax.psum_scatter(
            partial_out.astype(jnp.bfloat16), "tp", scatter_dimension=3, tiled=True
        )
        returned_parts.append(send_home(shares))
    returned = jnp.concatenate(returned_parts, axis=2)
    combined = jnp.dot(
        weight_rows, returned.reshape(slot_count, col_share).astype(jnp.float32), precision=highest
    )
    return (resid_cols + combined).astype(jnp.bfloat16)


def solution(mesh):
    in_specs = (
        P("req", None),
        P(),
        P(None, "tp"),
        P(None, "tp"),
        P(),
        P(None, "tp"),
        P(None, "tp"),
        P("tp", None),
        P(),
        P("req", None, "tp"),
        P("req", None, "tp"),
        P("req", "tp", None),
        P("req", None, None),
        P("req", None),
        P("req"),
        P("req", None, None),
        P("req", None),
        P("req", None),
    )
    out_specs = P("req", "tp")
    return jax.shard_map(local, mesh=mesh, in_specs=in_specs, out_specs=out_specs, check_vma=False)
```

profile of v0, /device:TPU:1, one launch (start us, length us, event | category | flops | bytes accessed | tf_op | source)
XLA Modules:
  0.0 439.2 jit_solution(9429141945775908812)
XLA Ops:
  9.4 1.6 fusion.199
  11.0 11.2 %all_gather.15 = f32[128,576]{0,1:T(8,128)S(1)} all-gather(f32[128,144]{0,1:T(8,128)S(1)} %fusion.199), channel_id=1, replica_groups=mesh['req'=64,'tp'=4] {'tp'}, dimensions={1}, use_global_device_ids=true | all-gather | bytes 368640 | tf_op jit(solution)/shard_map/all_gather | solution.py:93
  43.3 1.7 copy.232
  45.0 1.7 copy.231
  53.7 2.2 reshape.335
  55.9 3.0 fusion.227
  59.0 4.2 gather_fusion
  63.2 2.1 bitcast_select_fusion
  65.3 2.0 fusion.226
  67.4 2.5 reshape.337
  69.9 1.5 exponential_reduce_fusion
  73.2 1.9 fusion.185
  75.1 2.1 fusion.35
  78.1 2.0 copy.230
  81.7 3.0 fusion.228
  85.0 2.2 convert_element_type.135
  87.6 1.8 reduce-window.6
  92.3 22.1 %reduce-scatter.6.cloned.1.call-done = f32[128,512]{1,0:T(8,128)} async-done(((f32[128,2048]{1,0:T(8,128)}), f32[128,512]{1,0:T(8,128)}) %reduce-scatter.6.cloned.1.call-update) | async-done | bytes 262160 | tf_op jit(solution)/shard_map/reduce_scatter | solution.py:181
  115.6 6.5 %psum.7 = f32[128,1]{0,1:T(1,128)S(1)} all-reduce(f32[128,1]{0,1:T(1,128)S(1)} %bitcast.433), channel_id=1, replica_groups=mesh['req'=64,'tp'=4] {'tp'}, use_global_device_ids=true, to_apply=%region_13.14 | all-reduce | flops 128 | bytes 1024 | tf_op jit(solution)/shard_map/psum | solution.py:184
  122.1 1.8 convolution_convert_fusion
  125.3 31.6 %all_to_all.40 = bf16[64,1,6,512]{3,2,1,0:T(8,128)(2,1)S(1)} all-to-all(bf16[64,1,6,512]{3,2,1,0:T(8,128)(2,1)S(1)} %get-tuple-element.10), channel_id=1, replica_groups=mesh['req'=64,'tp'=4] {'req'}, dimensions={0} | all-to-all | bytes 786432 | tf_op jit(solution)/shard_map/all_to_all | solution.py:195
  157.9 23.4 %all_to_all.41 = bf16[64,1,6,512]{3,2,1,0:T(8,128)(2,1)S(1)} all-to-all(bf16[64,1,6,512]{3,2,1,0:T(8,128)(2,1)} %get-tuple-element.11), channel_id=1, replica_groups=mesh['req'=64,'tp'=4] {'req'}, dimensions={0} | all-to-all | bytes 786432 | tf_op jit(solution)/shard_map/all_to_all | solution.py:195
  182.3 23.4 %all_to_all.42 = bf16[64,1,6,512]{3,2,1,0:T(8,128)(2,1)S(1)} all-to-all(bf16[64,1,6,512]{3,2,1,0:T(8,128)(2,1)} %get-tuple-element.12), channel_id=1, replica_groups=mesh['req'=64,'tp'=4] {'req'}, dimensions={0} | all-to-all | bytes 786432 | tf_op jit(solution)/shard_map/all_to_all | solution.py:195
  206.7 23.4 %all_to_all.43 = bf16[64,1,6,512]{3,2,1,0:T(8,128)(2,1)S(1)} all-to-all(bf16[64,1,6,512]{3,2,1,0:T(8,128)(2,1)} %get-tuple-element.9), channel_id=1, replica_groups=mesh['req'=64,'tp'=4] {'req'}, dimensions={0} | all-to-all | bytes 786432 | tf_op jit(solution)/shard_map/all_to_all | solution.py:195
  231.1 3.7 fusion.81
  234.8 5.5 %fusion.3 = bf16[64,1,6,2048]{3,0,2,1:T(8,128)(2,1)} fusion(bf16[1,352,2048]{2,1,0:T(8,128)(2,1)} %param.29, bf16[1,2048,352]{1,2,0:T(8,128)(2,1)} %param.28, bf16[64,1,6,2048]{3,0,2,1:T(8,128)(2,1)} %all-gather.11.cloned.1.call-done, f32[64,1,6,352]{3,0,2,1:T(8,128)} %fusion.81), kind=kOutput, calls=%fused_computation.13 | convolution fusion | flops 1108893696 | bytes 6569984 | tf_op jit(solution)/shard_map/nesf,efd->nesd/dot_general | solution.py:39
  240.5 3.7 fusion.66
  244.2 5.5 %fusion.2 = bf16[64,1,6,2048]{3,0,2,1:T(8,128)(2,1)} fusion(bf16[1,352,2048]{2,1,0:T(8,128)(2,1)} %param.29, bf16[1,2048,352]{1,2,0:T(8,128)(2,1)} %param.28, bf16[64,1,6,2048]{3,0,2,1:T(8,128)(2,1)} %all-gather.9.cloned.1.call-done, f32[64,1,6,352]{3,0,2,1:T(8,128)} %fusion.66), kind=kOutput, calls=%fused_computation.12 | convolution fusion | flops 1108893696 | bytes 6569984 | tf_op jit(solution)/shard_map/nesf,efd->nesd/dot_general | solution.py:39
  250.0 3.7 fusion.51
  253.7 5.5 %fusion.1 = bf16[64,1,6,2048]{3,0,2,1:T(8,128)(2,1)} fusion(bf16[1,352,2048]{2,1,0:T(8,128)(2,1)} %param.29, bf16[1,2048,352]{1,2,0:T(8,128)(2,1)} %param.28, bf16[64,1,6,2048]{3,0,2,1:T(8,128)(2,1)} %all-gather.7.cloned.1.call-done, f32[64,1,6,352]{3,0,2,1:T(8,128)} %fusion.51), kind=kOutput, calls=%fused_computation.11 | convolution fusion | flops 1108893696 | bytes 6569984 | tf_op jit(solution)/shard_map/nesf,efd->nesd/dot_general | solution.py:39
  259.3 15.5 %all-gather.5.cloned.1.call-done = bf16[64,1,6,2048]{3,0,2,1:T(8,128)(2,1)} async-done(((bf16[64,1,6,512]{3,0,2,1:T(8,128)(2,1)}), bf16[64,1,6,2048]{3,0,2,1:T(8,128)(2,1)}) %all-gather.5.cloned.1.call-update) | async-done | bytes 1572880 | tf_op jit(solution)/shard_map/all_gather | solution.py:202
  274.8 3.7 fusion.36
  278.5 5.5 %fusion = bf16[64,1,6,2048]{3,0,2,1:T(8,128)(2,1)} fusion(bf16[1,352,2048]{2,1,0:T(8,128)(2,1)} %param.29, bf16[1,2048,352]{1,2,0:T(8,128)(2,1)} %param.28, bf16[64,1,6,2048]{3,0,2,1:T(8,128)(2,1)} %all-gather.5.cloned.1.call-done, f32[64,1,6,352]{3,0,2,1:T(8,128)} %fusion.36), kind=kOutput, calls=%fused_computation.10 | convolution fusion | flops 1108893696 | bytes 6569984 | tf_op jit(solution)/shard_map/nesf,efd->nesd/dot_general | solution.py:39
  284.0 20.7 %reduce-scatter.14.cloned.1.call-done = bf16[64,1,6,512]{3,0,2,1:T(8,128)(2,1)} async-done(((bf16[64,1,6,2048]{3,0,2,1:T(8,128)(2,1)}), bf16[64,1,6,512]{3,0,2,1:T(8,128)(2,1)}) %reduce-scatter.14.cloned.1.call-update) | async-done | bytes 393232 | tf_op jit(solution)/shard_map/reduce_scatter | solution.py:204
  304.7 2.0 copy.218
  306.8 11.9 %all-to-all-start.7 = ((bf16[64,1,6,512]{3,2,1,0:T(8,128)(2,1)}), bf16[64,1,6,512]{3,2,1,0:T(8,128)(2,1)}, u32[]{:S(2)}, u32[]{:S(2)}) async-start(bf16[64,1,6,512]{3,2,1,0:T(8,128)(2,1)} %copy.218), calls=%async_computation.12 | async-start | bytes 1048576 | tf_op jit(solution)/shard_map/all_to_all | solution.py:43
  318.6 16.8 %reduce-scatter.12.cloned.1.call-done = bf16[64,1,6,512]{3,0,2,1:T(8,128)(2,1)} async-done(((bf16[64,1,6,2048]{3,0,2,1:T(8,128)(2,1)}), bf16[64,1,6,512]{3,0,2,1:T(8,128)(2,1)}) %reduce-scatter.12.cloned.1.call-update) | async-done | bytes 393232 | tf_op jit(solution)/shard_map/reduce_scatter | solution.py:204
  335.5 2.0 copy.215
  337.5 11.9 %all-to-all-start.5 = ((bf16[64,1,6,512]{3,2,1,0:T(8,128)(2,1)}), bf16[64,1,6,512]{3,2,1,0:T(8,128)(2,1)}, u32[]{:S(2)}, u32[]{:S(2)}) async-start(bf16[64,1,6,512]{3,2,1,0:T(8,128)(2,1)} %copy.215), calls=%async_computation.9 | async-start | bytes 1048576 | tf_op jit(solution)/shard_map/all_to_all | solution.py:43
  349.4 16.9 %reduce-scatter.10.cloned.1.call-done = bf16[64,1,6,512]{3,0,2,1:T(8,128)(2,1)} async-done(((bf16[64,1,6,2048]{3,0,2,1:T(8,128)(2,1)}), bf16[64,1,6,512]{3,0,2,1:T(8,128)(2,1)}) %reduce-scatter.10.cloned.1.call-update) | async-done | bytes 393232 | tf_op jit(solution)/shard_map/reduce_scatter | solution.py:204
  366.2 2.0 copy.212
  368.2 12.0 %all-to-all-start.3 = ((bf16[64,1,6,512]{3,2,1,0:T(8,128)(2,1)}), bf16[64,1,6,512]{3,2,1,0:T(8,128)(2,1)}, u32[]{:S(2)}, u32[]{:S(2)}) async-start(bf16[64,1,6,512]{3,2,1,0:T(8,128)(2,1)} %copy.212), calls=%async_computation.6 | async-start | bytes 1048576 | tf_op jit(solution)/shard_map/all_to_all | solution.py:43
  380.3 16.7 %reduce-scatter.8.cloned.1.call-done = bf16[64,1,6,512]{3,0,2,1:T(8,128)(2,1)} async-done(((bf16[64,1,6,2048]{3,0,2,1:T(8,128)(2,1)}), bf16[64,1,6,512]{3,0,2,1:T(8,128)(2,1)}) %reduce-scatter.8.cloned.1.call-update) | async-done | bytes 393232 | tf_op jit(solution)/shard_map/reduce_scatter | solution.py:204
  397.0 2.0 copy.209
  399.0 11.9 %all-to-all-start.1 = ((bf16[64,1,6,512]{3,2,1,0:T(8,128)(2,1)}), bf16[64,1,6,512]{3,2,1,0:T(8,128)(2,1)}, u32[]{:S(2)}, u32[]{:S(2)}) async-start(bf16[64,1,6,512]{3,2,1,0:T(8,128)(2,1)} %copy.209), calls=%async_computation.3 | async-start | bytes 1048576 | tf_op jit(solution)/shard_map/all_to_all | solution.py:43
  410.9 1.5 select_reduce_fusion
  412.5 16.1 %all-to-all-done.1 = bf16[64,1,6,512]{3,2,1,0:T(8,128)(2,1)} async-done(((bf16[64,1,6,512]{3,2,1,0:T(8,128)(2,1)}), bf16[64,1,6,512]{3,2,1,0:T(8,128)(2,1)}, u32[]{:S(2)}, u32[]{:S(2)}) %all-to-all-start.1) | async-done | bytes 393248 | tf_op jit(solution)/shard_map/all_to_all | solution.py:43
  428.5 2.6 pad_maximum_fusion
  (147 shorter events, 47.0 us)
Async XLA Ops:
  6.5 34.7 %copy-start = (bf16[2048,768]{1,0:T(8,128)(2,1)S(1)}, bf16[2048,768]{1,0:T(8,128)(2,1)}, u32[]{:S(2)}) copy-start(bf16[2048,768]{1,0:T(8,128)(2,1)} %param.20) | copy-start | bytes 9437188
  6.5 17.9 %copy-start.14 = (f32[512]{0:T(512)S(1)}, f32[512]{0:T(512)}, u32[]{:S(2)}) copy-start(f32[512]{0:T(512)} %param.22) | copy-start | bytes 6148
  6.5 107.9 %reduce-scatter.6.cloned.1.call-start = ((), (), s32[]{:S(2)}) async-start(), calls=%async_computation.13 | async-start | bytes 1310720 | tf_op jit(solution)/shard_map/reduce_scatter | solution.py:181
  9.3 14.2 %copy-start.15 = (f32[128]{0:T(128)}, f32[128]{0:T(128)S(1)}, u32[]{:S(2)}) copy-start(f32[128]{0:T(128)S(1)} %add_rsqrt_fusion.1) | copy-start | bytes 1540
  9.4 17.3 %copy-start.12 = (s32[4,3,8]{2,0,1:T(4,128)S(1)}, s32[4,3,8]{2,0,1:T(4,128)}, u32[]{:S(2)}) copy-start(s32[4,3,8]{2,0,1:T(4,128)} %param.33) | copy-start | bytes 1156
  38.4 2.8 copy-start.3
  38.4 2.8 copy-start.10
  38.4 2.8 copy-start.16
  39.5 0.8 copy-start.7
  51.4 0.8 copy-start.6
  52.3 3.6 copy-start.17
  59.0 4.2 copy-start.11
  63.2 2.1 copy-start.5
  63.2 2.1 copy-start.9
  65.3 2.0 copy-start.1
  73.2 2.0 copy-start.2
  84.7 2.4 copy-start.8
  84.7 146.4 %all-gather.11.cloned.1.call-start = ((), (), s32[]{:S(2)}) async-start(), calls=%async_computation.20 | async-start | bytes 1966080 | tf_op jit(solution)/shard_map/all_gather | solution.py:202
  157.8 82.6 %all-gather.9.cloned.1.call-start = ((), (), s32[]{:S(2)}) async-start(), calls=%async_computation.18 | async-start | bytes 1966080 | tf_op jit(solution)/shard_map/all_gather | solution.py:202
  182.2 67.8 %all-gather.7.cloned.1.call-start = ((), (), s32[]{:S(2)}) async-start(), calls=%async_computation.16 | async-start | bytes 1966080 | tf_op jit(solution)/shard_map/all_gather | solution.py:202
  206.6 68.1 %all-gather.5.cloned.1.call-start = ((), (), s32[]{:S(2)}) async-start(), calls=%async_computation.14 | async-start | bytes 1966080 | tf_op jit(solution)/shard_map/all_gather | solution.py:202
  231.1 73.7 %reduce-scatter.14.cloned.1.call-start = ((), (), s32[]{:S(2)}) async-start(), calls=%async_computation.21 | async-start | bytes 1966080 | tf_op jit(solution)/shard_map/reduce_scatter | solution.py:204
  240.4 95.1 %reduce-scatter.12.cloned.1.call-start = ((), (), s32[]{:S(2)}) async-start(), calls=%async_computation.19 | async-start | bytes 1966080 | tf_op jit(solution)/shard_map/reduce_scatter | solution.py:204
  249.7 116.5 %reduce-scatter.10.cloned.1.call-start = ((), (), s32[]{:S(2)}) async-start(), calls=%async_computation.17 | async-start | bytes 1966080 | tf_op jit(solution)/shard_map/reduce_scatter | solution.py:204
  259.2 137.8 %reduce-scatter.8.cloned.1.call-start = ((), (), s32[]{:S(2)}) async-start(), calls=%async_computation.15 | async-start | bytes 1966080 | tf_op jit(solution)/shard_map/reduce_scatter | solution.py:204
  306.8 30.7 %all-to-all-start.7 = ((bf16[64,1,6,512]{3,2,1,0:T(8,128)(2,1)}), bf16[64,1,6,512]{3,2,1,0:T(8,128)(2,1)}, u32[]{:S(2)}, u32[]{:S(2)}) async-start(bf16[64,1,6,512]{3,2,1,0:T(8,128)(2,1)} %copy.218), calls=%async_computation.12 | async-start | bytes 1048576 | tf_op jit(solution)/shard_map/all_to_all | solution.py:43
  337.5 30.8 %all-to-all-start.5 = ((bf16[64,1,6,512]{3,2,1,0:T(8,128)(2,1)}), bf16[64,1,6,512]{3,2,1,0:T(8,128)(2,1)}, u32[]{:S(2)}, u32[]{:S(2)}) async-start(bf16[64,1,6,512]{3,2,1,0:T(8,128)(2,1)} %copy.215), calls=%async_computation.9 | async-start | bytes 1048576 | tf_op jit(solution)/shard_map/all_to_all | solution.py:43
  368.2 42.7 %copy-start.13 = (f32[128,6]{0,1:T(8,128)S(1)}, f32[128,6]{0,1:T(8,128)}, u32[]{:S(2)}) copy-start(f32[128,6]{0,1:T(8,128)} %param.35) | copy-start | bytes 9220
  368.2 30.8 %all-to-all-start.3 = ((bf16[64,1,6,512]{3,2,1,0:T(8,128)(2,1)}), bf16[64,1,6,512]{3,2,1,0:T(8,128)(2,1)}, u32[]{:S(2)}, u32[]{:S(2)}) async-start(bf16[64,1,6,512]{3,2,1,0:T(8,128)(2,1)} %copy.212), calls=%async_computation.6 | async-start | bytes 1048576 | tf_op jit(solution)/shard_map/all_to_all | solution.py:43
  399.0 29.5 %all-to-all-start.1 = ((bf16[64,1,6,512]{3,2,1,0:T(8,128)(2,1)}), bf16[64,1,6,512]{3,2,1,0:T(8,128)(2,1)}, u32[]{:S(2)}, u32[]{:S(2)}) async-start(bf16[64,1,6,512]{3,2,1,0:T(8,128)(2,1)} %copy.209), calls=%async_computation.3 | async-start | bytes 1048576 | tf_op jit(solution)/shard_map/all_to_all | solution.py:43
  428.5 2.6 copy-start.4
Sparse Core Ops, SparseCore 0:
  84.9 29.5 reduce-scatter.5
  157.9 23.6 all-gather.10
  183.6 29.1 all-gather.8
  214.6 29.1 all-gather.6
  245.6 29.1 all-gather.4
  277.3 27.3 reduce-scatter.13
  307.5 27.9 reduce-scatter.11
  338.2 27.9 reduce-scatter.9
  369.0 27.9 reduce-scatter.7
where the time goes:
time: 441 us; the launch traced here: 439 us
  waiting for transfers between devices  125 us (28%)
  blocking collectives  120 us (27%)
  matrix products  65.8 us (15%)
  starting transfers between devices  48.4 us (11%)
  local copies, waits for them, and re-layouts  39.7 us (9%)
  other arithmetic  27 us (6%)
  between operations  13.7 us (3%)
    all_to_all x4, blocking collectives, local(): lax.all_to_all(placed[:, :, chunk_index * chunk:(chunk_index + 1) * chunk...  102 us
    reduce_scatter x4, waiting for transfers between devices, local(): lax.psum_scatter(partial_out.astype(jnp.bfloat16), 'tp', scatter_dimensio...  71.2 us
    all_to_all x4, starting transfers between devices, send_home(): lax.all_to_all(shares, 'req', split_axis=0, concat_axis=0, tiled=True)  47.7 us
    reduce_scatter x1, waiting for transfers between devices, local(): lax.psum_scatter(attn_part, 'tp', scatter_dimension=1, tiled=True)  22.1 us
    dot_general x4, matrix products, expert_math(): jnp.einsum('nesf,efd->nesd', active, down_w, preferred_element_type=jnp.f...  22 us
    all_to_all x4, waiting for transfers between devices, send_home(): lax.all_to_all(shares, 'req', split_axis=0, concat_axis=0, tiled=True)  16.1 us
    all_gather x4, waiting for transfers between devices, local(): arrived = lax.all_gather(arrived_cols, 'tp', axis=3, tiled=True)  15.6 us
    dot_general x4, matrix products, expert_math(): jnp.einsum('nesd,edf->nesf', arrived, gate_w, preferred_element_type=jnp....  14.8 us
  transfers between devices with their start and end apart: 13, of which 7 were waited for; matrix products, arithmetic and copies ran while one was open for 13% of the time, Pallas kernels for 0%

commit v1 on v0

--- a/solution.py
+++ b/solution.py
@@ -90,7 +90,12 @@
         jnp.bfloat16
     )
     kv_part = jnp.dot(normed, w_latent, preferred_element_type=jnp.float32)
-    kv_all = lax.all_gather(kv_part, "tp", axis=1, tiled=True)
+    ring = [kv_part]
+    for hop in range(3):
+        ring.append(lax.ppermute(ring[-1], "tp", [(dev, (dev + 1) % 4) for dev in range(4)]))
+    kv_all = jnp.roll(
+        jnp.concatenate(ring[::-1], axis=1), (lax.axis_index("tp") + 1) * ring[0].shape[1], axis=1
+    )
     new_lat = kv_all[:, :LATENT] * rms_scale(kv_all[:, :LATENT]) * kv_gain
     new_rope = rotate(kv_all[:, LATENT:], cos_val, sin_val)
     new_keys = jnp.concatenate([new_lat, new_rope], axis=1).astype(jnp.bfloat16)

time: 441 us -> 438 us (level); the launches traced: 439 us -> 431 us
  waiting for transfers between devices: 125 us -> 140 us
  blocking collectives: 120 us -> 108 us
  matrix products: 65.8 us -> 56.9 us
  other arithmetic: 27 us -> 21.3 us
    all_gather x1 -> x0, blocking collectives: 11.2 us -> none  [local(): kv_all = lax.all_gather(kv_part, 'tp', axis=1, tiled=True)]
    ppermute x0 -> x3, waiting for transfers between devices: none -> 7.09 us  [local(): lax.ppermute(ring[-1], 'tp', [(dev, (dev + 1) % 4) for dev in range(4)])]
    all_gather x4, waiting for transfers between devices: 15.6 us -> 20.4 us  [local(): arrived = lax.all_gather(arrived_cols, 'tp', axis=3, tiled=True)]
  transfers between devices with their start and end apart: 13 -> 16, of which waited for: 7 -> 9; matrix products, arithmetic and copies ran while one was open for 13% -> 16% of each run, Pallas kernels for 0% -> 0%
where the time goes in v1:
time: 438 us; the launch traced here: 431 us
  waiting for transfers between devices  140 us (32%)
  blocking collectives  108 us (25%)
  matrix products  56.9 us (13%)
  starting transfers between devices  51.3 us (12%)
  local copies, waits for them, and re-layouts  40 us (9%)
  other arithmetic  21.3 us (5%)
  between operations  14.1 us (3%)
    all_to_all x4, blocking collectives, local(): lax.all_to_all(placed[:, :, chunk_index * chunk:(chunk_index + 1) * chunk...  102 us
    reduce_scatter x4, waiting for transfers between devices, local(): lax.psum_scatter(partial_out.astype(jnp.bfloat16), 'tp', scatter_dimensio...  72.9 us
    all_to_all x4, starting transfers between devices, send_home(): lax.all_to_all(shares, 'req', split_axis=0, concat_axis=0, tiled=True)  47.1 us
    reduce_scatter x1, waiting for transfers between devices, local(): lax.psum_scatter(attn_part, 'tp', scatter_dimension=1, tiled=True)  23 us
    all_gather x4, waiting for transfers between devices, local(): arrived = lax.all_gather(arrived_cols, 'tp', axis=3, tiled=True)  20.4 us
    dot_general x4, matrix products, expert_math(): jnp.einsum('nesf,efd->nesd', active, down_w, preferred_element_type=jnp.f...  19.5 us
    all_to_all x4, waiting for transfers between devices, send_home(): lax.all_to_all(shares, 'req', split_axis=0, concat_axis=0, tiled=True)  16.2 us
    dot_general x4, matrix products, expert_math(): jnp.einsum('nesd,edf->nesf', arrived, gate_w, preferred_element_type=jnp....  11.8 us
  transfers between devices with their start and end apart: 16, of which 9 were waited for; matrix products, arithmetic and copies ran while one was open for 16% of the time, Pallas kernels for 0%

profile of v1, /device:TPU:1, one launch (start us, length us, event | category | flops | bytes accessed | tf_op | source)
XLA Modules:
  0.0 431.3 jit_solution(14284850287529520054)
XLA Ops:
  8.0 1.6 fusion.199
  9.6 2.1 collective-permute-start
  15.5 2.5 fusion.200
  19.1 4.1 gather_fusion
  23.2 2.0 bitcast_select_fusion
  26.9 1.7 copy.231
  28.6 2.0 copy.230
  32.5 3.2 collective-permute-done.1
  36.6 3.9 collective-permute-done.2
  58.7 2.2 reshape.335
  60.9 3.0 fusion.227
  64.0 3.0 fusion.226
  67.2 2.5 reshape.337
  69.7 1.6 exponential_reduce_fusion
  73.0 1.7 fusion.185
  77.3 1.5 fusion.228
  79.9 1.8 reduce-window.6
  83.7 23.0 %reduce-scatter.6.cloned.1.call-done = f32[128,512]{1,0:T(8,128)} async-done(((f32[128,2048]{1,0:T(8,128)}), f32[128,512]{1,0:T(8,128)}) %reduce-scatter.6.cloned.1.call-update) | async-done | bytes 262160 | tf_op jit(solution)/shard_map/reduce_scatter | solution.py:186
  107.8 6.4 %psum.7 = f32[128,1]{0,1:T(1,128)S(1)} all-reduce(f32[128,1]{0,1:T(1,128)S(1)} %bitcast.437), channel_id=1, replica_groups=mesh['req'=64,'tp'=4] {'tp'}, use_global_device_ids=true, to_apply=%region_13.14 | all-reduce | flops 128 | bytes 1024 | tf_op jit(solution)/shard_map/psum | solution.py:189
  116.3 31.8 %all_to_all.40 = bf16[64,1,6,512]{3,2,1,0:T(8,128)(2,1)S(1)} all-to-all(bf16[64,1,6,512]{3,2,1,0:T(8,128)(2,1)S(1)} %get-tuple-element.10), channel_id=1, replica_groups=mesh['req'=64,'tp'=4] {'req'}, dimensions={0} | all-to-all | bytes 786432 | tf_op jit(solution)/shard_map/all_to_all | solution.py:200
  149.0 23.4 %all_to_all.41 = bf16[64,1,6,512]{3,2,1,0:T(8,128)(2,1)S(1)} all-to-all(bf16[64,1,6,512]{3,2,1,0:T(8,128)(2,1)S(1)} %copy-done.13), channel_id=1, replica_groups=mesh['req'=64,'tp'=4] {'req'}, dimensions={0} | all-to-all | bytes 786432 | tf_op jit(solution)/shard_map/all_to_all | solution.py:200
  173.3 23.2 %all_to_all.42 = bf16[64,1,6,512]{3,2,1,0:T(8,128)(2,1)S(1)} all-to-all(bf16[64,1,6,512]{3,2,1,0:T(8,128)(2,1)S(1)} %copy-done.12), channel_id=1, replica_groups=mesh['req'=64,'tp'=4] {'req'}, dimensions={0} | all-to-all | bytes 786432 | tf_op jit(solution)/shard_map/all_to_all | solution.py:200
  197.5 23.2 %all_to_all.43 = bf16[64,1,6,512]{3,2,1,0:T(8,128)(2,1)S(1)} all-to-all(bf16[64,1,6,512]{3,2,1,0:T(8,128)(2,1)S(1)} %get-tuple-element.9), channel_id=1, replica_groups=mesh['req'=64,'tp'=4] {'req'}, dimensions={0} | all-to-all | bytes 786432 | tf_op jit(solution)/shard_map/all_to_all | solution.py:200
  221.7 2.9 fusion.81
  224.7 4.9 %fusion.3 = bf16[64,1,6,2048]{3,0,2,1:T(8,128)(2,1)} fusion(bf16[1,352,2048]{2,1,0:T(8,128)(2,1)} %param.29, bf16[1,2048,352]{1,2,0:T(8,128)(2,1)} %param.28, bf16[64,1,6,2048]{3,0,2,1:T(8,128)(2,1)S(1)} %copy-done.34, f32[64,1,6,352]{3,0,2,1:T(8,128)S(1)} %fusion.81), kind=kOutput, calls=%fused_computation.13 | convolution fusion | flops 1108893696 | bytes 6569984 | tf_op jit(solution)/shard_map/nesf,efd->nesd/dot_general | solution.py:39
  229.6 3.0 fusion.66
  232.6 4.9 %fusion.2 = bf16[64,1,6,2048]{3,0,2,1:T(8,128)(2,1)} fusion(bf16[1,352,2048]{2,1,0:T(8,128)(2,1)} %param.29, bf16[1,2048,352]{1,2,0:T(8,128)(2,1)} %param.28, bf16[64,1,6,2048]{3,0,2,1:T(8,128)(2,1)S(1)} %copy-done.33, f32[64,1,6,352]{3,0,2,1:T(8,128)S(1)} %fusion.66), kind=kOutput, calls=%fused_computation.12 | convolution fusion | flops 1108893696 | bytes 6569984 | tf_op jit(solution)/shard_map/nesf,efd->nesd/dot_general | solution.py:39
  237.6 2.9 fusion.51
  240.6 4.9 %fusion.1 = bf16[64,1,6,2048]{3,0,2,1:T(8,128)(2,1)} fusion(bf16[1,352,2048]{2,1,0:T(8,128)(2,1)} %param.29, bf16[1,2048,352]{1,2,0:T(8,128)(2,1)} %param.28, bf16[64,1,6,2048]{3,0,2,1:T(8,128)(2,1)S(1)} %copy-done.32, f32[64,1,6,352]{3,0,2,1:T(8,128)S(1)} %fusion.51), kind=kOutput, calls=%fused_computation.11 | convolution fusion | flops 1108893696 | bytes 6569984 | tf_op jit(solution)/shard_map/nesf,efd->nesd/dot_general | solution.py:39
  245.5 20.3 %all-gather.5.cloned.1.call-done = bf16[64,1,6,2048]{3,0,2,1:T(8,128)(2,1)} async-done(((bf16[64,1,6,512]{3,0,2,1:T(8,128)(2,1)}), bf16[64,1,6,2048]{3,0,2,1:T(8,128)(2,1)}) %all-gather.5.cloned.1.call-update) | async-done | bytes 1572880 | tf_op jit(solution)/shard_map/all_gather | solution.py:207
  265.9 2.9 fusion.36
  268.8 4.9 %fusion = bf16[64,1,6,2048]{3,0,2,1:T(8,128)(2,1)} fusion(bf16[1,352,2048]{2,1,0:T(8,128)(2,1)} %param.29, bf16[1,2048,352]{1,2,0:T(8,128)(2,1)} %param.28, bf16[64,1,6,2048]{3,0,2,1:T(8,128)(2,1)S(1)} %copy-done.31, f32[64,1,6,352]{3,0,2,1:T(8,128)S(1)} %fusion.36), kind=kOutput, calls=%fused_computation.10 | convolution fusion | flops 1108893696 | bytes 6569984 | tf_op jit(solution)/shard_map/nesf,efd->nesd/dot_general | solution.py:39
  273.7 22.1 %reduce-scatter.14.cloned.1.call-done = bf16[64,1,6,512]{3,0,2,1:T(8,128)(2,1)} async-done(((bf16[64,1,6,2048]{3,0,2,1:T(8,128)(2,1)}), bf16[64,1,6,512]{3,0,2,1:T(8,128)(2,1)}) %reduce-scatter.14.cloned.1.call-update) | async-done | bytes 393232 | tf_op jit(solution)/shard_map/reduce_scatter | solution.py:209
  295.8 2.0 copy.218
  297.8 11.9 %all-to-all-start.7 = ((bf16[64,1,6,512]{3,2,1,0:T(8,128)(2,1)}), bf16[64,1,6,512]{3,2,1,0:T(8,128)(2,1)S(1)}, u32[]{:S(2)}, u32[]{:S(2)}) async-start(bf16[64,1,6,512]{3,2,1,0:T(8,128)(2,1)} %copy.218), calls=%async_computation.12 | async-start | bytes 1048576 | tf_op jit(solution)/shard_map/all_to_all | solution.py:43
  309.7 16.8 %reduce-scatter.12.cloned.1.call-done = bf16[64,1,6,512]{3,0,2,1:T(8,128)(2,1)} async-done(((bf16[64,1,6,2048]{3,0,2,1:T(8,128)(2,1)}), bf16[64,1,6,512]{3,0,2,1:T(8,128)(2,1)}) %reduce-scatter.12.cloned.1.call-update) | async-done | bytes 393232 | tf_op jit(solution)/shard_map/reduce_scatter | solution.py:209
  326.6 2.0 copy.215
  328.6 11.7 %all-to-all-start.5 = ((bf16[64,1,6,512]{3,2,1,0:T(8,128)(2,1)}), bf16[64,1,6,512]{3,2,1,0:T(8,128)(2,1)S(1)}, u32[]{:S(2)}, u32[]{:S(2)}) async-start(bf16[64,1,6,512]{3,2,1,0:T(8,128)(2,1)} %copy.215), calls=%async_computation.9 | async-start | bytes 1048576 | tf_op jit(solution)/shard_map/all_to_all | solution.py:43
  340.3 17.0 %reduce-scatter.10.cloned.1.call-done = bf16[64,1,6,512]{3,0,2,1:T(8,128)(2,1)} async-done(((bf16[64,1,6,2048]{3,0,2,1:T(8,128)(2,1)}), bf16[64,1,6,512]{3,0,2,1:T(8,128)(2,1)}) %reduce-scatter.10.cloned.1.call-update) | async-done | bytes 393232 | tf_op jit(solution)/shard_map/reduce_scatter | solution.py:209
  357.3 2.0 copy.212
  359.4 11.8 %all-to-all-start.3 = ((bf16[64,1,6,512]{3,2,1,0:T(8,128)(2,1)}), bf16[64,1,6,512]{3,2,1,0:T(8,128)(2,1)S(1)}, u32[]{:S(2)}, u32[]{:S(2)}) async-start(bf16[64,1,6,512]{3,2,1,0:T(8,128)(2,1)} %copy.212), calls=%async_computation.6 | async-start | bytes 1048576 | tf_op jit(solution)/shard_map/all_to_all | solution.py:43
  371.2 16.9 %reduce-scatter.8.cloned.1.call-done = bf16[64,1,6,512]{3,0,2,1:T(8,128)(2,1)} async-done(((bf16[64,1,6,2048]{3,0,2,1:T(8,128)(2,1)}), bf16[64,1,6,512]{3,0,2,1:T(8,128)(2,1)}) %reduce-scatter.8.cloned.1.call-update) | async-done | bytes 393232 | tf_op jit(solution)/shard_map/reduce_scatter | solution.py:209
  388.1 2.0 copy.209
  390.2 11.7 %all-to-all-start.1 = ((bf16[64,1,6,512]{3,2,1,0:T(8,128)(2,1)}), bf16[64,1,6,512]{3,2,1,0:T(8,128)(2,1)S(1)}, u32[]{:S(2)}, u32[]{:S(2)}) async-start(bf16[64,1,6,512]{3,2,1,0:T(8,128)(2,1)} %copy.209), calls=%async_computation.3 | async-start | bytes 1048576 | tf_op jit(solution)/shard_map/all_to_all | solution.py:43
  401.9 1.5 select_reduce_fusion
  403.4 16.2 %all-to-all-done.1 = bf16[64,1,6,512]{3,2,1,0:T(8,128)(2,1)S(1)} async-done(((bf16[64,1,6,512]{3,2,1,0:T(8,128)(2,1)}), bf16[64,1,6,512]{3,2,1,0:T(8,128)(2,1)S(1)}, u32[]{:S(2)}, u32[]{:S(2)}) %all-to-all-start.1) | async-done | bytes 393248 | tf_op jit(solution)/shard_map/all_to_all | solution.py:43
  420.4 2.7 pad_maximum_fusion
  423.1 1.5 fusion.138
  (197 shorter events, 44.1 us)
Async XLA Ops:
  6.5 9.0 %copy-start = (bf16[2048,768]{1,0:T(8,128)(2,1)S(1)}, bf16[2048,768]{1,0:T(8,128)(2,1)}, u32[]{:S(2)}) copy-start(bf16[2048,768]{1,0:T(8,128)(2,1)} %param.20) | copy-start | bytes 9437188
  6.5 9.0 %copy-start.26 = (f32[2048]{0:T(1024)S(1)}, f32[2048]{0:T(1024)}, u32[]{:S(2)}) copy-start(f32[2048]{0:T(1024)} %param.19) | copy-start | bytes 24580
  6.5 5.2 %copy-start.27 = (s32[4,3,8]{2,0,1:T(4,128)S(1)}, s32[4,3,8]{2,0,1:T(4,128)}, u32[]{:S(2)}) copy-start(s32[4,3,8]{2,0,1:T(4,128)} %param.33) | copy-start | bytes 1156
  6.5 6.3 %copy-start.30 = (s32[4]{0:T(128)S(1)}, s32[4]{0:T(128)}, u32[]{:S(2)}) copy-start(s32[4]{0:T(128)} %param.32) | copy-start | bytes 52
  6.5 7.0 %copy-start.29 = (s32[4,8]{1,0:T(4,128)S(1)}, s32[4,8]{1,0:T(4,128)}, u32[]{:S(2)}) copy-start(s32[4,8]{1,0:T(4,128)} %param.31) | copy-start | bytes 388
  6.5 100.2 %reduce-scatter.6.cloned.1.call-start = ((), (), s32[]{:S(2)}) async-start(), calls=%async_computation.13 | async-start | bytes 1310720 | tf_op jit(solution)/shard_map/reduce_scatter | solution.py:186
  9.6 21.6 %collective-permute-start = (f32[128,144]{0,1:T(8,128)S(1)}, f32[128,144]{0,1:T(8,128)S(1)}, u32[]{:S(2)}, u32[]{:S(2)}) collective-permute-start(f32[128,144]{0,1:T(8,128)S(1)} %fusion.199), channel_id=1, source_target_pairs={{0,1},{1,2},{2,3},{3,0},{4,5},{5,6},{6,7},{7,4},{8,9},{9,10},{10,1... | collective-permute-start | bytes 221192 | tf_op jit(solution)/shard_map/ppermute | solution.py:95
  11.8 1.0 copy-start.17
  12.0 6.0 %copy-start.20 = (f32[4,8,8]{2,1,0:T(8,128)}, f32[4,8,8]{2,1,0:T(8,128)S(1)}, u32[]{:S(2)}) copy-start(f32[4,8,8]{2,1,0:T(8,128)S(1)} %fusion.207) | copy-start | bytes 3076
  12.9 5.1 %copy-start.19 = (f32[4,8,8]{2,1,0:T(8,128)}, f32[4,8,8]{2,1,0:T(8,128)S(1)}, u32[]{:S(2)}) copy-start(f32[4,8,8]{2,1,0:T(8,128)S(1)} %fusion.205) | copy-start | bytes 3076
  14.8 3.3 copy-start.21
  15.5 3.2 copy-start.16
  31.3 4.4 %collective-permute-start.1 = (f32[128,144]{0,1:T(8,128)S(1)}, f32[128,144]{0,1:T(8,128)S(1)}, u32[]{:S(2)}, u32[]{:S(2)}) collective-permute-start(f32[128,144]{0,1:T(8,128)S(1)} %collective-permute-done), channel_id=1, source_target_pairs={{0,1},{1,2},{2,3},{3,0},{4,5},{5,6},{6,7},{7,4},{8,9},{9,10},{10,1... | collective-permute-start | bytes 221192 | tf_op jit(solution)/shard_map/ppermute | solution.py:95
  35.7 4.9 %collective-permute-start.2 = (f32[128,144]{0,1:T(8,128)S(1)}, f32[128,144]{0,1:T(8,128)S(1)}, u32[]{:S(2)}, u32[]{:S(2)}) collective-permute-start(f32[128,144]{0,1:T(8,128)S(1)} %collective-permute-done.1), channel_id=1, source_target_pairs={{0,1},{1,2},{2,3},{3,0},{4,5},{5,6},{6,7},{7,4},{8,9},{9,10},{10,1... | collective-permute-start | bytes 221192 | tf_op jit(solution)/shard_map/ppermute | solution.py:95
  40.6 6.6 %copy-start.18 = (f32[8,8]{1,0:T(8,128)S(1)}, f32[8,8]{1,0:T(8,128)}, u32[]{:S(2)}) copy-start(f32[8,8]{1,0:T(8,128)} %copy-done.17) | copy-start | bytes 772
  53.3 1.9 copy-start.22
  54.1 1.0 copy-start.23
  57.3 3.6 copy-start.35
  60.9 3.1 copy-start.25
  69.7 3.3 slice-start
  73.0 1.7 copy-start.14
  74.7 1.0 copy-start.11
  75.6 1.6 copy-start.10
  77.3 1.6 copy-start.2
  78.8 142.9 %all-gather.11.cloned.1.call-start = ((), (), s32[]{:S(2)}) async-start(), calls=%async_computation.20 | async-start | bytes 1966080 | tf_op jit(solution)/shard_map/all_gather | solution.py:207
  116.3 32.7 %copy-start.13 = (bf16[64,1,6,512]{3,2,1,0:T(8,128)(2,1)S(1)}, bf16[64,1,6,512]{3,2,1,0:T(8,128)(2,1)}, u32[]{:S(2)}) copy-start(bf16[64,1,6,512]{3,2,1,0:T(8,128)(2,1)} %get-tuple-element.11) | copy-start | bytes 1179652
  148.9 24.4 %copy-start.12 = (bf16[64,1,6,512]{3,2,1,0:T(8,128)(2,1)S(1)}, bf16[64,1,6,512]{3,2,1,0:T(8,128)(2,1)}, u32[]{:S(2)}) copy-start(bf16[64,1,6,512]{3,2,1,0:T(8,128)(2,1)} %get-tuple-element.12) | copy-start | bytes 1179652
  148.9 80.7 %all-gather.9.cloned.1.call-start = ((), (), s32[]{:S(2)}) async-start(), calls=%async_computation.18 | async-start | bytes 1966080 | tf_op jit(solution)/shard_map/all_gather | solution.py:207
  173.3 64.3 %all-gather.7.cloned.1.call-start = ((), (), s32[]{:S(2)}) async-start(), calls=%async_computation.16 | async-start | bytes 1966080 | tf_op jit(solution)/shard_map/all_gather | solution.py:207
  197.4 68.4 %all-gather.5.cloned.1.call-start = ((), (), s32[]{:S(2)}) async-start(), calls=%async_computation.14 | async-start | bytes 1966080 | tf_op jit(solution)/shard_map/all_gather | solution.py:207
  221.6 74.2 %reduce-scatter.14.cloned.1.call-start = ((), (), s32[]{:S(2)}) async-start(), calls=%async_computation.21 | async-start | bytes 1966080 | tf_op jit(solution)/shard_map/reduce_scatter | solution.py:209
  221.7 3.0 copy-start.34
  229.6 97.0 %reduce-scatter.12.cloned.1.call-start = ((), (), s32[]{:S(2)}) async-start(), calls=%async_computation.19 | async-start | bytes 1966080 | tf_op jit(solution)/shard_map/reduce_scatter | solution.py:209
  229.6 3.0 copy-start.33
  237.5 119.8 %reduce-scatter.10.cloned.1.call-start = ((), (), s32[]{:S(2)}) async-start(), calls=%async_computation.17 | async-start | bytes 1966080 | tf_op jit(solution)/shard_map/reduce_scatter | solution.py:209
  237.6 3.0 copy-start.32
  245.5 142.7 %reduce-scatter.8.cloned.1.call-start = ((), (), s32[]{:S(2)}) async-start(), calls=%async_computation.15 | async-start | bytes 1966080 | tf_op jit(solution)/shard_map/reduce_scatter | solution.py:209
  265.9 3.0 copy-start.31
  297.8 30.8 %all-to-all-start.7 = ((bf16[64,1,6,512]{3,2,1,0:T(8,128)(2,1)}), bf16[64,1,6,512]{3,2,1,0:T(8,128)(2,1)S(1)}, u32[]{:S(2)}, u32[]{:S(2)}) async-start(bf16[64,1,6,512]{3,2,1,0:T(8,128)(2,1)} %copy.218), calls=%async_computation.12 | async-start | bytes 1048576 | tf_op jit(solution)/shard_map/all_to_all | solution.py:43
  328.6 61.6 %copy-start.6 = (bf16[64,1,6,512]{3,2,1,0:T(8,128)(2,1)}, bf16[64,1,6,512]{3,2,1,0:T(8,128)(2,1)S(1)}, u32[]{:S(2)}) copy-start(bf16[64,1,6,512]{3,2,1,0:T(8,128)(2,1)S(1)} %all-to-all-done.7) | copy-start | bytes 1179652
  328.6 30.8 %all-to-all-start.5 = ((bf16[64,1,6,512]{3,2,1,0:T(8,128)(2,1)}), bf16[64,1,6,512]{3,2,1,0:T(8,128)(2,1)S(1)}, u32[]{:S(2)}, u32[]{:S(2)}) async-start(bf16[64,1,6,512]{3,2,1,0:T(8,128)(2,1)} %copy.215), calls=%async_computation.9 | async-start | bytes 1048576 | tf_op jit(solution)/shard_map/all_to_all | solution.py:43
  359.3 42.5 %copy-start.28 = (f32[128,6]{0,1:T(8,128)S(1)}, f32[128,6]{0,1:T(8,128)}, u32[]{:S(2)}) copy-start(f32[128,6]{0,1:T(8,128)} %param.35) | copy-start | bytes 9220
  359.4 44.0 %copy-start.7 = (bf16[64,1,6,512]{3,2,1,0:T(8,128)(2,1)}, bf16[64,1,6,512]{3,2,1,0:T(8,128)(2,1)S(1)}, u32[]{:S(2)}) copy-start(bf16[64,1,6,512]{3,2,1,0:T(8,128)(2,1)S(1)} %all-to-all-done.5) | copy-start | bytes 1179652
  359.4 30.8 %all-to-all-start.3 = ((bf16[64,1,6,512]{3,2,1,0:T(8,128)(2,1)}), bf16[64,1,6,512]{3,2,1,0:T(8,128)(2,1)S(1)}, u32[]{:S(2)}, u32[]{:S(2)}) async-start(bf16[64,1,6,512]{3,2,1,0:T(8,128)(2,1)} %copy.212), calls=%async_computation.6 | async-start | bytes 1048576 | tf_op jit(solution)/shard_map/all_to_all | solution.py:43
  390.2 29.4 %copy-start.8 = (bf16[64,1,6,512]{3,2,1,0:T(8,128)(2,1)}, bf16[64,1,6,512]{3,2,1,0:T(8,128)(2,1)S(1)}, u32[]{:S(2)}) copy-start(bf16[64,1,6,512]{3,2,1,0:T(8,128)(2,1)S(1)} %all-to-all-done.3) | copy-start | bytes 1179652
  390.2 29.4 %all-to-all-start.1 = ((bf16[64,1,6,512]{3,2,1,0:T(8,128)(2,1)}), bf16[64,1,6,512]{3,2,1,0:T(8,128)(2,1)S(1)}, u32[]{:S(2)}, u32[]{:S(2)}) async-start(bf16[64,1,6,512]{3,2,1,0:T(8,128)(2,1)} %copy.209), calls=%async_computation.3 | async-start | bytes 1048576 | tf_op jit(solution)/shard_map/all_to_all | solution.py:43
  420.4 2.7 copy-start.3
  420.4 4.2 copy-start.1
  (5 other events, 4.1 us)
Sparse Core Ops, SparseCore 0:
  78.9 27.7 reduce-scatter.5
  149.0 23.6 all-gather.10
  174.7 29.1 all-gather.8
  205.7 29.1 all-gather.6
  236.7 29.1 all-gather.4
  268.4 27.3 reduce-scatter.13
  298.5 27.9 reduce-scatter.11
  329.3 27.9 reduce-scatter.9
  360.1 28.0 reduce-scatter.7
